TPU v7x, 128 devices: a whole 4x4x4 slice. The times are simulated.
128 devices in a mesh: dof: 32 (over x, z, core), snap: 4 (over y).
Axes of the slice: x: 4, y: 4, z: 4, core: 2. Of those that a mesh axis runs over, the one named last changes fastest.
Arguments:
- snapshots: bfloat16 [131072, 1024], P('dof', 'snap')
- lengths: int32 [16], replicated, may hold values from 16 to 64, as said below
- start_block: float32 [1024, 128], replicated, may hold values from -6 to 6
Outputs:
- pod_modes: float32 [131072, 128], P(('dof', 'snap'))
- r_factor: float32 [1024, 1024], replicated
Inputs may be any that keep to these rules, and one draw needn't show every extreme that they name: `lengths`: some passage has all 64 steps active and some passage only a quarter of them.
All inputs are finite; a program needn't handle non-finite values.
Results may differ from a plain program's by a relative error of at most 0.0003.
Values may be sent and summed in bfloat16 or wider, within the bound.
No kernel may reach another device: no remote copies, remote signals or barrier semaphores. Data moves between devices by JAX's collectives and lax.ppermute only.
A program may use at most 128 MiB of HBM per device.

v0:
```python
import jax
import jax.numpy as jnp
from jax import lax
from jax.sharding import PartitionSpec as P

STEPS = 64
ITERS = 3
PASSES = 16


def body(snapshots, lengths, start_block):
    panel_width = snapshots.shape[1]
    first_col = lax.axis_index("snap") * panel_width
    columns = first_col + jnp.arange(panel_width, dtype=jnp.int32)
    passage = columns // STEPS
    lookup = passage[:, None] == jnp.arange(PASSES, dtype=jnp.int32)[None, :]
    col_length = jnp.sum(jnp.where(lookup, lengths[None, :], 0), axis=1)
    active = columns % STEPS < col_length
    masked = jnp.where(active[None, :], snapshots, jnp.zeros_like(snapshots))
    gathered_slab = lax.all_gather(masked, "snap", axis=1, tiled=True)
    row_count = gathered_slab.shape[0] * lax.axis_size("dof")
    contract = (((0,), (0,)), ((), ()))
    partial_gram = lax.dot_general(
        gathered_slab, gathered_slab, contract, preferred_element_type=jnp.float32
    )
    gram_sum = lax.psum(partial_gram, "dof")
    width = gram_sum.shape[0]
    shifted = gram_sum / jnp.float32(row_count) + 0.05 * jnp.eye(width, dtype=jnp.float32)
    upper_factor = jnp.linalg.cholesky(shifted).T
    subspace = start_block
    for sweep in range(ITERS):
        image = jnp.dot(
            shifted, subspace, precision=lax.Precision.HIGHEST, preferred_element_type=jnp.float32
        )
        correlation = lax.dot_general(
            image,
            image,
            contract,
            precision=lax.Precision.HIGHEST,
            preferred_element_type=jnp.float32,
        )
        lower_factor = jnp.linalg.cholesky(correlation)
        subspace = lax.linalg.triangular_solve(
            lower_factor, image, left_side=False, lower=True, transpose_a=True
        )
    quarter = gathered_slab.shape[0] // lax.axis_size("snap")
    own_rows = lax.dynamic_slice_in_dim(
        gathered_slab, lax.axis_index("snap") * quarter, quarter, 0
    ).astype(jnp.float32)
    pod_modes = jnp.dot(
        own_rows, subspace, precision=lax.Precision.HIGHEST, preferred_element_type=jnp.float32
    )
    return (pod_modes, upper_factor)


def solution(mesh):
    placed = (P("dof", "snap"), P(), P())
    return jax.shard_map(
        body, mesh=mesh, in_specs=placed, out_specs=(P(("dof", "snap"), None), P()), check_vma=False
    )
```

profile of v0, /device:TPU:1, one launch (start us, length us, event | category | flops | bytes accessed | tf_op | source)
XLA Modules:
  0.0 570.0 jit_solution(12406197987237153935)
XLA Ops:
  8.0 3.0 broadcast_select_fusion
  11.2 89.9 %all-gather.2.cloned.1.call-done = bf16[4096,1024]{1,0:T(8,128)(2,1)} async-done(((bf16[4096,256]{1,0:T(8,128)(2,1)}), bf16[4096,1024]{1,0:T(8,128)(2,1)}) %all-gather.2.cloned.1.call-update) | async-done | bytes 8388624 | tf_op jit(solution)/shard_map/all_gather | solution.py:20
  101.0 15.0 %fusion.79 = f32[1024,1024]{0,1:T(8,128)} fusion(bf16[4096,1024]{1,0:T(8,128)(2,1)} %all-gather.2.cloned.1.call-done), kind=kOutput, calls=%fused_computation.138 | convolution fusion | flops 8589934592 | bytes 12582912 | tf_op jit(solution)/shard_map/dot_general | solution.py:23
  116.1 113.1 %all-reduce.3.cloned.1.call-done = f32[1024,1024]{0,1:T(8,128)} async-done(((f32[1024,1024]{0,1:T(8,128)}), f32[1024,1024]{0,1:T(8,128)}) %all-reduce.3.cloned.1.call-update) | async-done | bytes 4194320 | tf_op jit(solution)/shard_map/psum | solution.py:26
  229.2 5.1 select_add_fusion
  234.3 5.8 %copy.29 = f32[1024,1024]{1,0:T(8,128)} copy(f32[1024,1024]{0,1:T(8,128)} %select_add_fusion) | data formatting | bytes 8388608 | tf_op jit(solution)/shard_map/add | solution.py:28
  240.1 4.5 fusion
  244.6 2.0 copy-done.2
  246.6 11.7 %cholesky.247 = f32[128,128]{1,0:T(8,128)S(1)} custom-call(f32[128,128]{1,0:T(8,128)S(1)} %cholesky.667), custom_call_target="Cholesky" | custom-call | tf_op jit(solution)/shard_map/jit(cholesky)/cholesky | solution.py:29
  258.5 9.8 %custom-call.64 = f32[1,128,128]{1,2,0:T(8,128)S(1)} custom-call(f32[1,128,128]{2,1,0:T(8,128)S(1)} %get-tuple-element.17), custom_call_target="InvertDiagBlocksLowerTriangular" | custom-call | tf_op jit(solution)/shard_map/jit(cholesky)/cholesky | solution.py:29
  268.3 1.5 fusion.9
  269.8 1.5 convolution_subtract_fusion
  271.6 11.7 %cholesky.270 = f32[128,128]{1,0:T(8,128)S(1)} custom-call(f32[128,128]{1,0:T(8,128)S(1)} %cholesky.671), custom_call_target="Cholesky" | custom-call | tf_op jit(solution)/shard_map/jit(cholesky)/cholesky | solution.py:29
  283.6 9.8 %custom-call.65 = f32[1,128,128]{1,2,0:T(8,128)S(1)} custom-call(f32[1,128,128]{2,1,0:T(8,128)S(1)} %get-tuple-element.15), custom_call_target="InvertDiagBlocksLowerTriangular" | custom-call | tf_op jit(solution)/shard_map/jit(cholesky)/cholesky | solution.py:29
  294.5 1.9 copy-done.1
  296.5 2.4 convolution_subtract_fusion.1
  298.9 11.7 %cholesky.493 = f32[128,128]{1,0:T(8,128)S(1)} custom-call(f32[128,128]{1,0:T(8,128)S(1)} %cholesky.676), custom_call_target="Cholesky" | custom-call | tf_op jit(solution)/shard_map/jit(cholesky)/cholesky | solution.py:29
  311.4 9.8 %custom-call.66 = f32[1,128,128]{1,2,0:T(8,128)S(1)} custom-call(f32[1,128,128]{2,1,0:T(8,128)S(1)} %get-tuple-element.13), custom_call_target="InvertDiagBlocksLowerTriangular" | custom-call | tf_op jit(solution)/shard_map/jit(cholesky)/cholesky | solution.py:29
  321.2 1.2 convolution_dynamic-update-slice_fusion.1
  322.5 3.3 convolution_subtract_fusion.2
  325.8 11.7 %cholesky.512 = f32[128,128]{1,0:T(8,128)S(1)} custom-call(f32[128,128]{1,0:T(8,128)S(1)} %cholesky.681), custom_call_target="Cholesky" | custom-call | tf_op jit(solution)/shard_map/jit(cholesky)/cholesky | solution.py:29
  338.3 9.8 %custom-call.67 = f32[1,128,128]{1,2,0:T(8,128)S(1)} custom-call(f32[1,128,128]{2,1,0:T(8,128)S(1)} %get-tuple-element.11), custom_call_target="InvertDiagBlocksLowerTriangular" | custom-call | tf_op jit(solution)/shard_map/jit(cholesky)/cholesky | solution.py:29
  348.1 1.1 convolution_dynamic-update-slice_fusion.2
  349.3 3.1 convolution_subtract_fusion.3
  352.4 12.1 %cholesky.531 = f32[128,128]{1,0:T(8,128)S(1)} custom-call(f32[128,128]{1,0:T(8,128)S(1)} %cholesky.686), custom_call_target="Cholesky" | custom-call | tf_op jit(solution)/shard_map/jit(cholesky)/cholesky | solution.py:29
  365.3 9.8 %custom-call.68 = f32[1,128,128]{1,2,0:T(8,128)S(1)} custom-call(f32[1,128,128]{2,1,0:T(8,128)S(1)} %get-tuple-element.9), custom_call_target="InvertDiagBlocksLowerTriangular" | custom-call | tf_op jit(solution)/shard_map/jit(cholesky)/cholesky | solution.py:29
  375.1 1.1 convolution_dynamic-update-slice_fusion.3
  376.2 3.1 convolution_subtract_fusion.4
  379.4 11.7 %cholesky.551 = f32[128,128]{1,0:T(8,128)S(1)} custom-call(f32[128,128]{1,0:T(8,128)S(1)} %cholesky.691), custom_call_target="Cholesky" | custom-call | tf_op jit(solution)/shard_map/jit(cholesky)/cholesky | solution.py:29
  391.9 9.8 %custom-call.69 = f32[1,128,128]{1,2,0:T(8,128)S(1)} custom-call(f32[1,128,128]{2,1,0:T(8,128)S(1)} %get-tuple-element.7), custom_call_target="InvertDiagBlocksLowerTriangular" | custom-call | tf_op jit(solution)/shard_map/jit(cholesky)/cholesky | solution.py:29
  402.7 2.8 convolution_subtract_fusion.5
  405.5 11.7 %cholesky.571 = f32[128,128]{1,0:T(8,128)S(1)} custom-call(f32[128,128]{1,0:T(8,128)S(1)} %cholesky.696), custom_call_target="Cholesky" | custom-call | tf_op jit(solution)/shard_map/jit(cholesky)/cholesky | solution.py:29
  418.0 9.8 %custom-call.70 = f32[1,128,128]{1,2,0:T(8,128)S(1)} custom-call(f32[1,128,128]{2,1,0:T(8,128)S(1)} %get-tuple-element.5), custom_call_target="InvertDiagBlocksLowerTriangular" | custom-call | tf_op jit(solution)/shard_map/jit(cholesky)/cholesky | solution.py:29
  428.7 2.1 convolution_subtract_fusion.6
  430.9 11.7 %cholesky.589 = f32[128,128]{1,0:T(8,128)S(1)} custom-call(f32[128,128]{1,0:T(8,128)S(1)} %convolution_subtract_fusion.6), custom_call_target="Cholesky" | custom-call | tf_op jit(solution)/shard_map/jit(cholesky)/cholesky | solution.py:29
  442.7 9.0 %fusion.78 = f32[1024,128]{1,0:T(8,128)S(1)} fusion(f32[1024,128]{1,0:T(8,128)S(1)} %copy-done, f32[1024,1024]{0,1:T(8,128)} %all-reduce.3.cloned.1.call-done), kind=kOutput, calls=%fused_computation.137 | convolution fusion | flops 1614807040 | bytes 5242880 | tf_op jit(solution)/shard_map/dot_general | solution.py:32
  451.7 1.0 fusion.80
  452.9 11.7 %cholesky.636 = f32[128,128]{1,0:T(8,128)S(1)} custom-call(f32[128,128]{1,0:T(8,128)S(1)} %fusion.38), custom_call_target="Cholesky" | custom-call | tf_op jit(solution)/shard_map/jit(cholesky)/cholesky | solution.py:42
  465.9 9.8 %custom-call.73 = f32[1,128,128]{1,2,0:T(8,128)S(1)} custom-call(f32[1,128,128]{2,1,0:T(8,128)S(1)} %fusion.21), custom_call_target="InvertDiagBlocksLowerTriangular" | custom-call | tf_op jit(solution)/shard_map/triangular_solve/custom-call.16 | solution.py:43
  476.4 9.2 %fusion.77 = f32[1024,128]{1,0:T(8,128)S(1)} fusion(f32[1024,128]{0,1:T(8,128)S(1)} %convolution_bitcast_fusion.2, f32[1024,1024]{0,1:T(8,128)} %all-reduce.3.cloned.1.call-done), kind=kOutput, calls=%fused_computation.136 | convolution fusion | flops 1614807040 | bytes 5242880 | tf_op jit(solution)/shard_map/dot_general | solution.py:32
  485.6 1.0 fusion.81
  486.7 11.7 %cholesky.647 = f32[128,128]{1,0:T(8,128)S(1)} custom-call(f32[128,128]{1,0:T(8,128)S(1)} %fusion.36), custom_call_target="Cholesky" | custom-call | tf_op jit(solution)/shard_map/jit(cholesky)/cholesky | solution.py:42
  499.8 9.8 %custom-call.74 = f32[1,128,128]{1,2,0:T(8,128)S(1)} custom-call(f32[1,128,128]{2,1,0:T(8,128)S(1)} %fusion.22), custom_call_target="InvertDiagBlocksLowerTriangular" | custom-call | tf_op jit(solution)/shard_map/triangular_solve/custom-call.16 | solution.py:43
  510.3 9.0 %fusion.76 = f32[1024,128]{1,0:T(8,128)S(1)} fusion(f32[1024,128]{0,1:T(8,128)S(1)} %convolution_bitcast_fusion.1, f32[1024,1024]{0,1:T(8,128)} %all-reduce.3.cloned.1.call-done), kind=kOutput, calls=%fused_computation.135 | convolution fusion | flops 1614807040 | bytes 5242880 | tf_op jit(solution)/shard_map/dot_general | solution.py:32
  520.3 11.7 %cholesky.658 = f32[128,128]{1,0:T(8,128)S(1)} custom-call(f32[128,128]{1,0:T(8,128)S(1)} %fusion.34), custom_call_target="Cholesky" | custom-call | tf_op jit(solution)/shard_map/jit(cholesky)/cholesky | solution.py:42
  533.4 9.8 %custom-call.75 = f32[1,128,128]{1,2,0:T(8,128)S(1)} custom-call(f32[1,128,128]{2,1,0:T(8,128)S(1)} %fusion.23), custom_call_target="InvertDiagBlocksLowerTriangular" | custom-call | tf_op jit(solution)/shard_map/triangular_solve/custom-call.16 | solution.py:43
  553.9 4.9 select_bitcast_fusion
  558.8 4.2 fusion.1
  (73 shorter events, 21.0 us)
Async XLA Ops:
  7.2 435.6 %copy-start = (f32[1024,128]{1,0:T(8,128)S(1)}, f32[1024,128]{1,0:T(8,128)}, u32[]{:S(2)}) copy-start(f32[1024,128]{1,0:T(8,128)} %param.8) | copy-start | bytes 1572868
  7.2 93.9 %all-gather.2.cloned.1.call-start = ((), (), s32[]{:S(2)}) async-start(), calls=%async_computation | async-start | bytes 10485760 | tf_op jit(solution)/shard_map/all_gather | solution.py:20
  11.1 218.1 %all-reduce.3.cloned.1.call-start = ((), (), s32[]{:S(2)}) async-start(), calls=%async_computation.1 | async-start | bytes 8388608 | tf_op jit(solution)/shard_map/psum | solution.py:26
  244.6 2.0 copy-start.2
  294.5 2.0 copy-start.1
Sparse Core Ops, SparseCore 0:
  11.2 89.7 all-gather.1
  116.2 112.9 all-reduce.2
where the time goes:
time: 575 us; the launch traced here: 570 us
  other arithmetic  254 us (44%)
  waiting for transfers between devices  203 us (35%)
  matrix products  77.3 us (13%)
  between operations  19.6 us (3%)
  local copies, waits for them, and re-layouts  15.6 us (3%)
    another operation x30, other arithmetic, body(): upper_factor = jnp.linalg.cholesky(shifted).T  167 us
    psum x1, waiting for transfers between devices, body(): gram_sum = lax.psum(partial_gram, 'dof')  113 us
    all_gather x1, waiting for transfers between devices, body(): gathered_slab = lax.all_gather(masked, 'snap', axis=1, tiled=True)  89.9 us
    another operation x9, other arithmetic, body(): lower_factor = jnp.linalg.cholesky(correlation)  37.2 us
    another operation x6, other arithmetic, body(): lax.linalg.triangular_solve(lower_factor, image, left_side=False, lower=T...  31.4 us
    dot_general x3, matrix products, body(): jnp.dot(shifted, subspace, precision=lax.Precision.HIGHEST, preferred_ele...  27.2 us
    another operation x14, matrix products, body(): upper_factor = jnp.linalg.cholesky(shifted).T  25.9 us
    dot_general x1, matrix products, body(): lax.dot_general(gathered_slab, gathered_slab, contract, preferred_element...  15 us
  transfers between devices with their start and end apart: 2, of which 2 were waited for; matrix products, arithmetic and copies ran while one was open for 0% of the time, Pallas kernels for 0%

commit v1 on v0

--- a/solution.py
+++ b/solution.py
@@ -1,11 +1,26 @@
+import functools
 import jax
 import jax.numpy as jnp
 from jax import lax
 from jax.sharding import PartitionSpec as P
+from jax.lax import all_to_all, axis_size
 
 STEPS = 64
 ITERS = 3
 PASSES = 16
+
+
+def wall_draft(inner_x, across):
+    n_peers_all = axis_size(across)
+    y2 = range(inner_x.ndim)
+    a_next = map(lambda to_i: n_peers_all if to_i == 1 else 1, y2)
+    inbox = list(a_next)
+    frame_out = jnp.tile(inner_x, inbox)
+    w2 = all_to_all(frame_out, split_axis=1, axis_name=across, tiled=True, concat_axis=1)
+    return w2
+
+
+arrange_results = functools.partial(wall_draft, across="snap")
 
 
 def body(snapshots, lengths, start_block):
@@ -17,7 +32,7 @@
     col_length = jnp.sum(jnp.where(lookup, lengths[None, :], 0), axis=1)
     active = columns % STEPS < col_length
     masked = jnp.where(active[None, :], snapshots, jnp.zeros_like(snapshots))
-    gathered_slab = lax.all_gather(masked, "snap", axis=1, tiled=True)
+    gathered_slab = arrange_results(masked)
     row_count = gathered_slab.shape[0] * lax.axis_size("dof")
     contract = (((0,), (0,)), ((), ()))
     partial_gram = lax.dot_general(

time: 575 us -> 596 us (1.037)
  blocking collectives: 0 us -> 97.8 us
  waiting for transfers between devices: 203 us -> 114 us
  local copies, waits for them, and re-layouts: 15.6 us -> 27.5 us
    all_to_all x0 -> x1, blocking collectives: none -> 97.8 us  [wall_draft(): all_to_all(frame_out, split_axis=1, axis_name=across, tiled=True, concat_...]
    all_gather x1 -> x0, waiting for transfers between devices: 89.9 us -> none  [body(): gathered_slab = lax.all_gather(masked, 'snap', axis=1, tiled=True)]
    all_to_all x0 -> x1, local copies, waits for them, and re-layouts: none -> 11.3 us  [wall_draft(): all_to_all(frame_out, split_axis=1, axis_name=across, tiled=True, concat_...]
  transfers between devices with their start and end apart: 2 -> 1, of which waited for: 2 -> 1; matrix products, arithmetic and copies ran while one was open for 0% -> 0% of each run, Pallas kernels for 0% -> 0%
where the time goes in v1:
time: 596 us; the launch traced here: 590 us
  other arithmetic  253 us (42%)
  waiting for transfers between devices  114 us (19%)
  blocking collectives  97.8 us (16%)
  matrix products  78.7 us (13%)
  local copies, waits for them, and re-layouts  27.5 us (5%)
  between operations  19.6 us (3%)
    another operation x30, other arithmetic, body(): upper_factor = jnp.linalg.cholesky(shifted).T  168 us
    psum x1, waiting for transfers between devices, body(): gram_sum = lax.psum(partial_gram, 'dof')  114 us
    all_to_all x1, blocking collectives, wall_draft(): all_to_all(frame_out, split_axis=1, axis_name=across, tiled=True, concat_...  97.8 us
    another operation x9, other arithmetic, body(): lower_factor = jnp.linalg.cholesky(correlation)  37.2 us
    another operation x6, other arithmetic, body(): lax.linalg.triangular_solve(lower_factor, image, left_side=False, lower=T...  31.4 us
    dot_general x3, matrix products, body(): jnp.dot(shifted, subspace, precision=lax.Precision.HIGHEST, preferred_ele...  27.2 us
    another operation x14, matrix products, body(): upper_factor = jnp.linalg.cholesky(shifted).T  25.9 us
    dot_general x1, matrix products, body(): lax.dot_general(gathered_slab, gathered_slab, contract, preferred_element...  15.9 us
  transfers between devices with their start and end apart: 1, of which 1 were waited for; matrix products, arithmetic and copies ran while one was open for 0% of the time, Pallas kernels for 0%

profile of v1, /device:TPU:1, one launch (start us, length us, event | category | flops | bytes accessed | tf_op | source)
XLA Modules:
  0.0 590.2 jit_solution(10818100573725221655)
XLA Ops:
  8.0 1.7 broadcast_select_fusion
  10.3 97.8 %all_to_all.9 = bf16[4096,4,256]{2,0,1:T(8,128)(2,1)} all-to-all(bf16[4096,4,256]{2,0,1:T(8,128)(2,1)S(1)} %tile.2), channel_id=1, replica_groups=mesh['dof'=32,'snap'=4] {'snap'}, dimensions={1} | all-to-all | bytes 16777216 | tf_op jit(solution)/shard_map/all_to_all | solution.py:19
  108.1 11.3 %copy.66 = bf16[4096,4,256]{0,2,1:T(8,128)(2,1)} copy(bf16[4096,4,256]{2,0,1:T(8,128)(2,1)} %all_to_all.9) | data formatting | bytes 16777216 | tf_op jit(solution)/shard_map/all_to_all | solution.py:19
  119.4 15.9 %fusion.79 = f32[1024,1024]{0,1:T(8,128)} fusion(bf16[4096,1024]{0,1:T(8,128)(2,1)} %bitcast.91), kind=kOutput, calls=%fused_computation.138 | convolution fusion | flops 8589934592 | bytes 12582912 | tf_op jit(solution)/shard_map/dot_general | solution.py:38
  135.4 113.5 %all-reduce.3.cloned.1.call-done = f32[1024,1024]{0,1:T(8,128)} async-done(((f32[1024,1024]{0,1:T(8,128)}), f32[1024,1024]{0,1:T(8,128)}) %all-reduce.3.cloned.1.call-update) | async-done | bytes 4194320 | tf_op jit(solution)/shard_map/psum | solution.py:41
  248.9 5.1 select_add_fusion
  253.9 5.8 copy.71
  259.8 4.5 fusion
  264.2 2.0 copy-done.2
  266.3 11.7 %cholesky.247 = f32[128,128]{1,0:T(8,128)S(1)} custom-call(f32[128,128]{1,0:T(8,128)S(1)} %cholesky.667), custom_call_target="Cholesky" | custom-call | tf_op jit(solution)/shard_map/jit(cholesky)/cholesky | solution.py:44
  278.1 9.8 %custom-call.64 = f32[1,128,128]{1,2,0:T(8,128)S(1)} custom-call(f32[1,128,128]{2,1,0:T(8,128)S(1)} %get-tuple-element.17), custom_call_target="InvertDiagBlocksLowerTriangular" | custom-call | tf_op jit(solution)/shard_map/jit(cholesky)/cholesky | solution.py:44
  287.9 1.5 fusion.9
  289.5 1.6 convolution_subtract_fusion
  291.2 11.7 %cholesky.270 = f32[128,128]{1,0:T(8,128)S(1)} custom-call(f32[128,128]{1,0:T(8,128)S(1)} %cholesky.671), custom_call_target="Cholesky" | custom-call | tf_op jit(solution)/shard_map/jit(cholesky)/cholesky | solution.py:44
  303.2 9.8 %custom-call.65 = f32[1,128,128]{1,2,0:T(8,128)S(1)} custom-call(f32[1,128,128]{2,1,0:T(8,128)S(1)} %get-tuple-element.15), custom_call_target="InvertDiagBlocksLowerTriangular" | custom-call | tf_op jit(solution)/shard_map/jit(cholesky)/cholesky | solution.py:44
  314.2 1.9 copy-done.1
  316.1 2.4 convolution_subtract_fusion.1
  318.6 11.7 %cholesky.493 = f32[128,128]{1,0:T(8,128)S(1)} custom-call(f32[128,128]{1,0:T(8,128)S(1)} %cholesky.676), custom_call_target="Cholesky" | custom-call | tf_op jit(solution)/shard_map/jit(cholesky)/cholesky | solution.py:44
  331.1 9.8 %custom-call.66 = f32[1,128,128]{1,2,0:T(8,128)S(1)} custom-call(f32[1,128,128]{2,1,0:T(8,128)S(1)} %get-tuple-element.13), custom_call_target="InvertDiagBlocksLowerTriangular" | custom-call | tf_op jit(solution)/shard_map/jit(cholesky)/cholesky | solution.py:44
  340.9 1.2 convolution_dynamic-update-slice_fusion.1
  342.1 3.3 convolution_subtract_fusion.2
  345.4 11.7 %cholesky.512 = f32[128,128]{1,0:T(8,128)S(1)} custom-call(f32[128,128]{1,0:T(8,128)S(1)} %cholesky.681), custom_call_target="Cholesky" | custom-call | tf_op jit(solution)/shard_map/jit(cholesky)/cholesky | solution.py:44
  357.9 9.8 %custom-call.67 = f32[1,128,128]{1,2,0:T(8,128)S(1)} custom-call(f32[1,128,128]{2,1,0:T(8,128)S(1)} %get-tuple-element.11), custom_call_target="InvertDiagBlocksLowerTriangular" | custom-call | tf_op jit(solution)/shard_map/jit(cholesky)/cholesky | solution.py:44
  367.8 1.1 convolution_dynamic-update-slice_fusion.2
  368.9 3.1 convolution_subtract_fusion.3
  372.1 12.1 %cholesky.531 = f32[128,128]{1,0:T(8,128)S(1)} custom-call(f32[128,128]{1,0:T(8,128)S(1)} %cholesky.686), custom_call_target="Cholesky" | custom-call | tf_op jit(solution)/shard_map/jit(cholesky)/cholesky | solution.py:44
  384.9 9.8 %custom-call.68 = f32[1,128,128]{1,2,0:T(8,128)S(1)} custom-call(f32[1,128,128]{2,1,0:T(8,128)S(1)} %get-tuple-element.9), custom_call_target="InvertDiagBlocksLowerTriangular" | custom-call | tf_op jit(solution)/shard_map/jit(cholesky)/cholesky | solution.py:44
  394.8 1.1 convolution_dynamic-update-slice_fusion.3
  395.9 3.1 convolution_subtract_fusion.4
  399.0 11.7 %cholesky.551 = f32[128,128]{1,0:T(8,128)S(1)} custom-call(f32[128,128]{1,0:T(8,128)S(1)} %cholesky.691), custom_call_target="Cholesky" | custom-call | tf_op jit(solution)/shard_map/jit(cholesky)/cholesky | solution.py:44
  411.5 9.8 %custom-call.69 = f32[1,128,128]{1,2,0:T(8,128)S(1)} custom-call(f32[1,128,128]{2,1,0:T(8,128)S(1)} %get-tuple-element.7), custom_call_target="InvertDiagBlocksLowerTriangular" | custom-call | tf_op jit(solution)/shard_map/jit(cholesky)/cholesky | solution.py:44
  422.3 2.8 convolution_subtract_fusion.5
  425.1 11.7 %cholesky.571 = f32[128,128]{1,0:T(8,128)S(1)} custom-call(f32[128,128]{1,0:T(8,128)S(1)} %cholesky.696), custom_call_target="Cholesky" | custom-call | tf_op jit(solution)/shard_map/jit(cholesky)/cholesky | solution.py:44
  437.6 9.8 %custom-call.70 = f32[1,128,128]{1,2,0:T(8,128)S(1)} custom-call(f32[1,128,128]{2,1,0:T(8,128)S(1)} %get-tuple-element.5), custom_call_target="InvertDiagBlocksLowerTriangular" | custom-call | tf_op jit(solution)/shard_map/jit(cholesky)/cholesky | solution.py:44
  448.4 2.1 convolution_subtract_fusion.6
  450.5 11.7 %cholesky.589 = f32[128,128]{1,0:T(8,128)S(1)} custom-call(f32[128,128]{1,0:T(8,128)S(1)} %convolution_subtract_fusion.6), custom_call_target="Cholesky" | custom-call | tf_op jit(solution)/shard_map/jit(cholesky)/cholesky | solution.py:44
  462.4 9.0 %fusion.78 = f32[1024,128]{1,0:T(8,128)S(1)} fusion(f32[1024,128]{1,0:T(8,128)S(1)} %copy-done, f32[1024,1024]{0,1:T(8,128)} %all-reduce.3.cloned.1.call-done), kind=kOutput, calls=%fused_computation.137 | convolution fusion | flops 1614807040 | bytes 5242880 | tf_op jit(solution)/shard_map/dot_general | solution.py:47
  471.4 1.0 fusion.80
  472.5 11.7 %cholesky.636 = f32[128,128]{1,0:T(8,128)S(1)} custom-call(f32[128,128]{1,0:T(8,128)S(1)} %fusion.38), custom_call_target="Cholesky" | custom-call | tf_op jit(solution)/shard_map/jit(cholesky)/cholesky | solution.py:57
  485.5 9.8 %custom-call.73 = f32[1,128,128]{1,2,0:T(8,128)S(1)} custom-call(f32[1,128,128]{2,1,0:T(8,128)S(1)} %fusion.21), custom_call_target="InvertDiagBlocksLowerTriangular" | custom-call | tf_op jit(solution)/shard_map/triangular_solve/custom-call.16 | solution.py:58
  496.0 9.2 %fusion.77 = f32[1024,128]{1,0:T(8,128)S(1)} fusion(f32[1024,128]{0,1:T(8,128)S(1)} %convolution_bitcast_fusion.2, f32[1024,1024]{0,1:T(8,128)} %all-reduce.3.cloned.1.call-done), kind=kOutput, calls=%fused_computation.136 | convolution fusion | flops 1614807040 | bytes 5242880 | tf_op jit(solution)/shard_map/dot_general | solution.py:47
  506.4 11.7 %cholesky.647 = f32[128,128]{1,0:T(8,128)S(1)} custom-call(f32[128,128]{1,0:T(8,128)S(1)} %fusion.36), custom_call_target="Cholesky" | custom-call | tf_op jit(solution)/shard_map/jit(cholesky)/cholesky | solution.py:57
  519.4 9.8 %custom-call.74 = f32[1,128,128]{1,2,0:T(8,128)S(1)} custom-call(f32[1,128,128]{2,1,0:T(8,128)S(1)} %fusion.22), custom_call_target="InvertDiagBlocksLowerTriangular" | custom-call | tf_op jit(solution)/shard_map/triangular_solve/custom-call.16 | solution.py:58
  529.9 9.0 %fusion.76 = f32[1024,128]{1,0:T(8,128)S(1)} fusion(f32[1024,128]{0,1:T(8,128)S(1)} %convolution_bitcast_fusion.1, f32[1024,1024]{0,1:T(8,128)} %all-reduce.3.cloned.1.call-done), kind=kOutput, calls=%fused_computation.135 | convolution fusion | flops 1614807040 | bytes 5242880 | tf_op jit(solution)/shard_map/dot_general | solution.py:47
  540.0 11.7 %cholesky.658 = f32[128,128]{1,0:T(8,128)S(1)} custom-call(f32[128,128]{1,0:T(8,128)S(1)} %fusion.34), custom_call_target="Cholesky" | custom-call | tf_op jit(solution)/shard_map/jit(cholesky)/cholesky | solution.py:57
  553.0 9.8 %custom-call.75 = f32[1,128,128]{1,2,0:T(8,128)S(1)} custom-call(f32[1,128,128]{2,1,0:T(8,128)S(1)} %fusion.23), custom_call_target="InvertDiagBlocksLowerTriangular" | custom-call | tf_op jit(solution)/shard_map/triangular_solve/custom-call.16 | solution.py:58
  568.0 4.7 fusion.1
  578.2 4.9 select_bitcast_fusion
  (73 shorter events, 22.5 us)
Async XLA Ops:
  7.2 455.2 %copy-start = (f32[1024,128]{1,0:T(8,128)S(1)}, f32[1024,128]{1,0:T(8,128)}, u32[]{:S(2)}) copy-start(f32[1024,128]{1,0:T(8,128)} %param.8) | copy-start | bytes 1572868
  7.2 241.7 %all-reduce.3.cloned.1.call-start = ((), (), s32[]{:S(2)}) async-start(), calls=%async_computation.1 | async-start | bytes 8388608 | tf_op jit(solution)/shard_map/psum | solution.py:41
  264.2 2.0 copy-start.2
  314.2 2.0 copy-start.1
Sparse Core Ops, SparseCore 0:
  135.5 113.3 all-reduce.2
